TPU v7x, 32 devices: a whole 2x2x4 slice. The times are simulated.
32 devices in a mesh: gx: 8 (over z, core), gy: 4 (over y, x).
Axes of the slice: x: 2, y: 2, z: 4, core: 2. Of those that a mesh axis runs over, the one named last changes fastest.
Arguments:
- pressure: float32 [256, 128, 512], P('gx', 'gy'), may hold values from -6 to 6
- vel_x: float32 [256, 128, 512], P('gx', 'gy'), may hold values from -3 to 3
- vel_y: float32 [256, 128, 512], P('gx', 'gy'), may hold values from -3 to 3
- vel_z: float32 [256, 128, 512], P('gx', 'gy'), may hold values from -3 to 3
- void_frac: float32 [256, 128, 512], P('gx', 'gy'), may hold values from 1e-05 to 0.001
- waves: bfloat16 [24576, 2, 512], P(('gx', 'gy')), may hold values from -6 to 6
- bubble_dest: int32 [24576, 1], P(('gx', 'gy')), may hold values from 0 to 31; in each aligned block of 768 rows (0 to 767, 768 to 1535, ...) at most 48 rows name the same one
- bubble_column: int32 [24576], P(('gx', 'gy')), may hold values from 0 to 1023
- history: bfloat16 [128, 128, 512], P('gx', 'gy'), may hold values from -3 to 3
- delays: int32 [8, 8], replicated, may hold values from 0 to 15
Outputs:
- pressure_out: float32 [256, 128, 512], P('gx', 'gy')
- vel_x_out: float32 [256, 128, 512], P('gx', 'gy')
- vel_y_out: float32 [256, 128, 512], P('gx', 'gy')
- vel_z_out: float32 [256, 128, 512], P('gx', 'gy')
Inputs may be any that keep to these rules, and one draw needn't show every extreme that they name: `bubble_dest`: among the 768 bubbles listed on one device (an aligned block of rows), no tile is named more than 48 times.
All inputs are finite; a program needn't handle non-finite values.
Results may differ from a plain program's by a relative error of at most 0.00045.
Values may be sent and summed in bfloat16 or wider, within the bound.
No kernel may reach another device: no remote copies, remote signals or barrier semaphores. Data moves between devices by JAX's collectives and lax.ppermute only.
A program may use at most 128 MiB of HBM per device.

v0:
```python
import jax
import jax.numpy as jnp
from jax import lax
from jax.sharding import PartitionSpec as P

step_ratio = 0.4
gas_density = 0.001
gas_stiffness = 5.29e-05


def from_behind(block, axis, distance):
    devices = range(lax.axis_size(axis))
    route = [(i - distance, i) for i in devices if i - distance in devices]
    return lax.ppermute(block, axis, route)


def material(void_frac):
    liquid = 1.0 - void_frac
    buoyancy = 1.0 / (liquid + void_frac * gas_density)
    stiffness = 1.0 / (liquid + void_frac / gas_stiffness)
    return (buoyancy, stiffness)


def bubble_source(waves, bubble_dest, bubble_column, cells, ready):
    tiles_x = lax.axis_size("gx")
    tiles_y = lax.axis_size("gy")
    devices = tiles_x * tiles_y
    bubbles = waves.shape[0]
    steps = waves.shape[1]
    depth = waves.shape[2]
    capacity = 2 * bubbles // devices
    slots = devices * capacity
    me = lax.axis_index("gx") * tiles_y + lax.axis_index("gy")
    dest = bubble_dest[:, 0]
    owners = (dest[:, None] == jnp.arange(devices, dtype=jnp.int32)[None, :]).astype(jnp.int32)
    rank = jnp.sum(jnp.cumsum(owners, axis=0) * owners, axis=1) - 1
    slot_ids = dest * capacity + rank
    placed = slot_ids[None, :] == jnp.arange(slots, dtype=jnp.int32)[:, None]
    outgoing = jnp.dot(
        placed.astype(jnp.bfloat16),
        waves.reshape(bubbles, steps * depth),
        preferred_element_type=jnp.float32,
    ).astype(jnp.bfloat16)
    code = dest * cells + bubble_column
    all_code = lax.all_gather(code, ("gx", "gy"), axis=0, tiled=True).reshape(devices, bubbles)
    all_dest = all_code // cells
    all_col = all_code % cells
    mine = (all_dest == me).astype(jnp.int32)
    in_rank = jnp.cumsum(mine, axis=1) - 1
    in_rank = jnp.where(mine > 0, in_rank, -1)
    slot_of = jnp.arange(capacity, dtype=jnp.int32)
    match = in_rank[:, None, :] == slot_of[None, :, None]
    in_cols = jnp.max(jnp.where(match, all_col[:, None, :] + 1, 0), axis=2) - 1
    in_cols, outgoing, ready = lax.optimization_barrier((in_cols, outgoing, ready))
    incoming = lax.all_to_all(
        outgoing.reshape(devices, capacity, steps * depth),
        ("gx", "gy"),
        split_axis=0,
        concat_axis=0,
        tiled=True,
    )
    hits = (jnp.arange(cells, dtype=jnp.int32)[:, None] == in_cols.reshape(slots)[None, :]).astype(
        jnp.bfloat16
    )
    source = jnp.dot(
        hits, incoming.reshape(slots, steps * depth), preferred_element_type=jnp.float32
    )
    return (source, ready)


def incident_plane(history, delays, size_y, depth):
    tiles_x = lax.axis_size("gx")
    my_tile = lax.axis_index("gx")
    cycle = jnp.arange(tiles_x, dtype=jnp.int32)
    dist = jnp.abs(cycle - my_tile)
    dist = jnp.minimum(dist, tiles_x - dist)
    weight = 1.0 / (1.0 + 2.0 * dist.astype(jnp.float32) / tiles_x)
    wanted = lax.dynamic_index_in_dim(delays, my_tile, 1, keepdims=False)
    chosen = jnp.take(history, wanted, axis=0)
    rows = lax.all_to_all(chosen, "gx", split_axis=0, concat_axis=0, tiled=True)
    return jnp.sum(weight[:, None, None] * rows.astype(jnp.float32), axis=0)


def body(
    pressure, vel_x, vel_y, vel_z, void_frac, waves, bubble_dest, bubble_column, history, delays
):
    size_x, size_y, depth = pressure.shape
    steps = waves.shape[1]
    ix = lax.axis_index("gx")
    iy = lax.axis_index("gy")
    has_below_x = ix > 0
    has_below_y = iy > 0
    buoyancy, stiffness = material(void_frac)
    above_x = from_behind(pressure[0:1], "gx", -1)
    above_y = from_behind(pressure[:, 0:1], "gy", -1)
    below_x = from_behind(jnp.concatenate([pressure[-1:], vel_x[-1:], void_frac[-1:]], 0), "gx", 1)
    below_y = from_behind(
        jnp.concatenate([pressure[:, -1:], vel_y[:, -1:], void_frac[:, -1:]], 1), "gy", 1
    )
    incident = incident_plane(history, delays, size_y, depth)
    ready = (above_x, above_y, below_x, below_y, incident)
    source, ready = bubble_source(waves, bubble_dest, bubble_column, size_x * size_y, ready)
    above_x, above_y, below_x, below_y, incident = ready
    source = source.reshape(size_x, size_y, steps, depth)
    p_bx, vx_bx, void_bx = (below_x[0:1], below_x[1:2], below_x[2:3])
    p_by, vy_by, void_by = (below_y[:, 0:1], below_y[:, 1:2], below_y[:, 2:3])
    b_bx, _ = material(void_bx)
    b_by, _ = material(void_by)
    forcing = jnp.zeros_like(pressure).at[0].set(incident)
    z_edge = jnp.zeros((size_x, size_y, 1), jnp.float32)
    for step in range(steps):
        next_x = jnp.concatenate([pressure[1:], above_x], 0)
        next_y = jnp.concatenate([pressure[:, 1:], above_y], 1)
        next_z = jnp.concatenate([pressure[:, :, 1:], z_edge], 2)
        vel_x = vel_x - step_ratio * buoyancy * (next_x - pressure)
        vel_y = vel_y - step_ratio * buoyancy * (next_y - pressure)
        vel_z = vel_z - step_ratio * buoyancy * (next_z - pressure)
        vx_bx = vx_bx - step_ratio * b_bx * (pressure[0:1] - p_bx)
        vy_by = vy_by - step_ratio * b_by * (pressure[:, 0:1] - p_by)
        lower_x = jnp.where(has_below_x, vx_bx, 0.0)
        lower_y = jnp.where(has_below_y, vy_by, 0.0)
        prev_x = jnp.concatenate([lower_x, vel_x[:-1]], 0)
        prev_y = jnp.concatenate([lower_y, vel_y[:, :-1]], 1)
        prev_z = jnp.concatenate([z_edge, vel_z[:, :, :-1]], 2)
        divergence = vel_x - prev_x + (vel_y - prev_y) + (vel_z - prev_z)
        pressure = pressure + step_ratio * stiffness * (
            source[:, :, step, :] + forcing - divergence
        )
        if step + 1 < steps:
            above_x = from_behind(pressure[0:1], "gx", -1)
            above_y = from_behind(pressure[:, 0:1], "gy", -1)
            p_bx = from_behind(pressure[-1:], "gx", 1)
            p_by = from_behind(pressure[:, -1:], "gy", 1)
    return (pressure, vel_x, vel_y, vel_z)


def solution(mesh):
    in_specs = (
        P("gx", "gy", None),
        P("gx", "gy", None),
        P("gx", "gy", None),
        P("gx", "gy", None),
        P("gx", "gy", None),
        P(("gx", "gy"), None, None),
        P(("gx", "gy"), None),
        P(("gx", "gy")),
        P("gx", "gy", None),
        P(),
    )
    out_specs = (P("gx", "gy", None), P("gx", "gy", None), P("gx", "gy", None), P("gx", "gy", None))
    return jax.shard_map(body, mesh=mesh, in_specs=in_specs, out_specs=out_specs, check_vma=False)
```

profile of v0, /device:TPU:0, one launch (start us, length us, event | category | flops | bytes accessed | tf_op | source)
XLA Modules:
  0.0 215.8 jit_solution(4152463765882377466)
XLA Ops:
  0.7 1.4 fusion.50
  2.0 1.3 collective-permute-start.1
  7.3 3.2 %collective-permute-start.2 = (f32[3,32,512]{2,1,0:T(8,128)S(1)}, f32[3,32,512]{2,1,0:T(8,128)S(1)}, u32[]{:S(2)}, u32[]{:S(2)}) collective-permute-start(f32[3,32,512]{2,1,0:T(8,128)S(1)} %pad_maximum_fusion.1), channel_id=1, source_target_pairs={{0,4},{4,8},{8,12},{12,16},{16,20},{20,24},{24,28},{1,5},{5,9},{9,... | collective-permute-start | bytes 589832 | tf_op jit(solution)/shard_map/ppermute | solution.py:14
  13.6 6.3 %all-to-all-start = ((bf16[8,32,512]{2,1,0:T(8,128)(2,1)}), bf16[8,32,512]{2,1,0:T(8,128)(2,1)S(1)}, u32[]{:S(2)}, u32[]{:S(2)}) async-start(bf16[8,32,512]{2,1,0:T(8,128)(2,1)} %broadcast_select_fusion), calls=%async_computation | async-start | bytes 524288 | tf_op jit(solution)/shard_map/all_to_all | solution.py:80
  22.3 4.6 %collective-permute-start.3 = (f32[32,3,512]{2,1,0:T(4,128)S(1)}, f32[32,3,512]{2,1,0:T(4,128)S(1)}, u32[]{:S(2)}, u32[]{:S(2)}) collective-permute-start(f32[32,3,512]{2,1,0:T(4,128)S(1)} %pad_maximum_fusion), channel_id=1, source_target_pairs={{0,1},{1,2},{2,3},{4,5},{5,6},{6,7},{8,9},{9,10},{10,11},{12,13},{... | collective-permute-start | bytes 589832 | tf_op jit(solution)/shard_map/ppermute | solution.py:14
  26.9 1.7 reduce-window.16
  29.1 67.1 %all-gather = s32[32,1,768]{2,1,0:T(1,128)S(1)} all-gather(s32[1,1,768]{2,1,0:T(1,128)S(1)} %reshape.220), channel_id=1, replica_groups=mesh['gx'=8,'gy'=4] {'gx','gy'}, dimensions={0}, use_global_device_ids=true | all-gather | bytes 101376 | tf_op jit(solution)/shard_map/all_gather | solution.py:45
  96.5 1.7 reduce-window.14
  99.1 4.0 %fusion.4 = bf16[1536,1024]{1,0:T(8,128)(2,1)} fusion(bf16[768,1024]{1,0:T(8,128)(2,1)S(1)} %bitcast.129, s32[768]{0:T(1024)S(1)} %get-tuple-element.55), kind=kOutput, calls=%fused_computation.8 | convolution fusion | flops 2418671616 | bytes 4721664 | tf_op jit(solution)/shard_map/dot_general | solution.py:39
  104.1 3.9 %all-to-all-start.1 = ((bf16[32,48,1024]{2,1,0:T(8,128)(2,1)}), bf16[32,48,1024]{2,1,0:T(8,128)(2,1)}, u32[]{:S(2)}, u32[]{:S(2)}) async-start(bf16[32,48,1024]{2,1,0:T(8,128)(2,1)} %bitcast.126), calls=%async_computation.1 | async-start | bytes 6291456 | tf_op jit(solution)/shard_map/all_to_all | solution.py:55
  108.0 1.5 slice.148
  109.6 1.7 slice.153
  111.3 1.9 slice.158
  113.3 7.7 %multiply_subtract_fusion.1 = (f32[32,32,512]{2,1,0:T(8,128)}, f32[32,32,512]{2,1,0:T(8,128)}, f32[32,32,512]{2,1,0:T(8,128)S(1)}) fusion(f32[32,32,512]{2,1,0:T(8,128)} %param.15, f32[32,32,512]{2,1,0:T(8,128)S(1)} %copy-done.2, f32[32,32,511]{2,1,0:T(8,128)} %slice.158, f32[32,32,512]{2,1,0:T(8,128)} %param.16, f32[32,32,512]{2,1,0:T(8,128)} %param.14, ...), kind=kLoop, calls=%fused_computation.41 | loop fusion | flops 8388608 | bytes 23064576 | tf_op jit(solution)/shard_map/sub | solution.py:117
  121.0 1.6 slice.176
  123.2 55.8 %all-to-all-done.1 = bf16[32,48,1024]{2,1,0:T(8,128)(2,1)} async-done(((bf16[32,48,1024]{2,1,0:T(8,128)(2,1)}), bf16[32,48,1024]{2,1,0:T(8,128)(2,1)}, u32[]{:S(2)}, u32[]{:S(2)}) %all-to-all-start.1) | async-done | bytes 3145760 | tf_op jit(solution)/shard_map/all_to_all | solution.py:55
  179.0 4.7 %copy.38 = bf16[1536,1024]{0,1:T(8,128)(2,1)} copy(bf16[1536,1024]{1,0:T(8,128)(2,1)} %bitcast.4) | data formatting | bytes 6291456 | tf_op jit(solution)/shard_map/reshape | solution.py:66
  183.7 5.5 %fusion = f32[32,32,2,512]{3,1,2,0:T(8,128)S(1)} fusion(bf16[2,512,1536,1]{2,1,0,3:T(8,128)(2,1)} %bitcast.127, s32[1536]{0:T(1024)S(1)} %eq.113, s32[32,32]{1,0:T(8,128)S(1)} %multiply_add_fusion), kind=kOutput, calls=%fused_computation.1 | convolution fusion | flops 3222798336 | bytes 7350272 | tf_op jit(solution)/shard_map/dot_general | solution.py:65
  192.6 2.5 %fusion.14 = f32[32,32,512]{2,1,0:T(8,128)S(1)} fusion(f32[32,32,512]{2,1,0:T(8,128)S(1)} %copy-done.2, f32[32,32,512]{2,1,0:T(8,128)S(1)} %get-tuple-element.36, f32[32,32,512]{2,1,0:T(8,128)S(1)} %copy-done.7, f32[31,32,512]{2,1,0:T(8,128)S(1)} %copy-done.11, f32[1,32,512]{2,1,0:T(8,128)S(1)} %get-tuple-element.33, f32[32,32,512]{2,1,0:T(8,128)S(1)} %copy-done.5, ...), kind=kLoop, calls=%fused_computation.22 | loop fusion | flops 7864320 | bytes 20967424 | tf_op jit(solution)/shard_map/add | solution.py:126
  195.2 1.5 collective-permute-start.5
  196.8 3.4 %collective-permute-start.7 = (f32[32,1,512]{2,1,0:T(1,128)S(1)}, f32[32,1,512]{2,1,0:T(1,128)S(1)}, u32[]{:S(2)}, u32[]{:S(2)}) collective-permute-start(f32[32,1,512]{2,1,0:T(1,128)S(1)} %slice.186), channel_id=1, source_target_pairs={{0,1},{1,2},{2,3},{4,5},{5,6},{6,7},{8,9},{9,10},{10,11},{12,13},{... | collective-permute-start | bytes 196616 | tf_op jit(solution)/shard_map/ppermute | solution.py:14
  204.8 4.0 %collective-permute-done.6 = f32[32,1,512]{2,1,0:T(1,128)S(1)} collective-permute-done((f32[32,1,512]{2,1,0:T(1,128)S(1)}, f32[32,1,512]{2,1,0:T(1,128)S(1)}, u32[]{:S(2)}, u32[]{:S(2)}) %collective-permute-start.6) | collective-permute-done | bytes 65568 | tf_op jit(solution)/shard_map/ppermute | solution.py:14
  208.8 2.8 %multiply_subtract_fusion = (f32[32,32,512]{2,1,0:T(8,128)S(1)}, f32[32,32,512]{2,1,0:T(8,128)S(1)}, f32[32,32,512]{2,1,0:T(8,128)S(1)}) fusion(f32[32,32,512]{2,1,0:T(8,128)S(1)} %copy-done.4, f32[32,32,512]{2,1,0:T(8,128)S(1)} %fusion.14, f32[32,32,511]{2,1,0:T(8,128)S(1)} %slice.188, f32[32,32,512]{2,1,0:T(8,128)S(1)} %copy-done.3, ...), kind=kLoop, calls=%fused_computation.40 | loop fusion | flops 8388608 | bytes 23064576 | tf_op jit(solution)/shard_map/sub | solution.py:117
  211.9 3.6 %fusion.23 = f32[32,32,512]{2,1,0:T(8,128)} fusion(f32[32,32,512]{2,1,0:T(8,128)S(1)} %fusion.14, f32[32,32,512]{2,1,0:T(8,128)S(1)} %get-tuple-element.35, f32[32,32,512]{2,1,0:T(8,128)S(1)} %get-tuple-element.39, f32[31,32,512]{2,1,0:T(8,128)S(1)} %slice.183, f32[1,32,512]{2,1,0:T(8,128)S(1)} %get-tuple-element.47, ...), kind=kLoop, calls=%fused_computation.35 | loop fusion | flops 7864320 | bytes 20967424 | tf_op jit(solution)/shard_map/add | solution.py:126
  (84 shorter events, 20.9 us)
Async XLA Ops:
  0.6 11.6 %copy-start = (bf16[16,32,512]{2,1,0:T(8,128)(2,1)S(1)}, bf16[16,32,512]{2,1,0:T(8,128)(2,1)}, u32[]{:S(2)}) copy-start(bf16[16,32,512]{2,1,0:T(8,128)(2,1)} %param.20) | copy-start | bytes 1572868
  0.6 26.2 %copy-start.14 = (s32[768,1]{0,1:T(1,128)S(1)}, s32[768,1]{0,1:T(1,128)}, u32[]{:S(2)}) copy-start(s32[768,1]{0,1:T(1,128)} %param.18) | copy-start | bytes 9220
  0.7 28.4 %copy-start.13 = (s32[768]{0:T(1024)S(1)}, s32[768]{0:T(1024)}, u32[]{:S(2)}) copy-start(s32[768]{0:T(1024)} %param.19) | copy-start | bytes 9220
  2.0 102.0 %collective-permute-start.1 = (f32[32,1,512]{2,1,0:T(1,128)S(1)}, f32[32,1,512]{2,1,0:T(1,128)S(1)}, u32[]{:S(2)}, u32[]{:S(2)}) collective-permute-start(f32[32,1,512]{2,1,0:T(1,128)S(1)} %get-tuple-element.50), channel_id=1, source_target_pairs={{1,0},{2,1},{3,2},{5,4},{6,5},{7,6},{9,8},{10,9},{11,10},{13,12},{... | collective-permute-start | bytes 196616 | tf_op jit(solution)/shard_map/ppermute | solution.py:14
  4.2 99.9 %collective-permute-start = (f32[1,32,512]{2,1,0:T(8,128)S(1)}, f32[1,32,512]{2,1,0:T(8,128)S(1)}, u32[]{:S(2)}, u32[]{:S(2)}) collective-permute-start(f32[1,32,512]{2,1,0:T(8,128)S(1)} %get-tuple-element.52), channel_id=1, source_target_pairs={{4,0},{8,4},{12,8},{16,12},{20,16},{24,20},{28,24},{5,1},{9,5},{13... | collective-permute-start | bytes 196616 | tf_op jit(solution)/shard_map/ppermute | solution.py:14
  7.2 91.5 %copy-start.12 = (bf16[768,2,512]{2,1,0:T(2,128)(2,1)S(1)}, bf16[768,2,512]{2,1,0:T(2,128)(2,1)}, u32[]{:S(2)}) copy-start(bf16[768,2,512]{2,1,0:T(2,128)(2,1)} %param.17) | copy-start | bytes 4718596
  7.3 96.9 %collective-permute-start.2 = (f32[3,32,512]{2,1,0:T(8,128)S(1)}, f32[3,32,512]{2,1,0:T(8,128)S(1)}, u32[]{:S(2)}, u32[]{:S(2)}) collective-permute-start(f32[3,32,512]{2,1,0:T(8,128)S(1)} %pad_maximum_fusion.1), channel_id=1, source_target_pairs={{0,4},{4,8},{8,12},{12,16},{16,20},{20,24},{24,28},{1,5},{5,9},{9,... | collective-permute-start | bytes 589832 | tf_op jit(solution)/shard_map/ppermute | solution.py:14
  13.6 90.4 %all-to-all-start = ((bf16[8,32,512]{2,1,0:T(8,128)(2,1)}), bf16[8,32,512]{2,1,0:T(8,128)(2,1)S(1)}, u32[]{:S(2)}, u32[]{:S(2)}) async-start(bf16[8,32,512]{2,1,0:T(8,128)(2,1)} %broadcast_select_fusion), calls=%async_computation | async-start | bytes 524288 | tf_op jit(solution)/shard_map/all_to_all | solution.py:80
  22.3 81.8 %collective-permute-start.3 = (f32[32,3,512]{2,1,0:T(4,128)S(1)}, f32[32,3,512]{2,1,0:T(4,128)S(1)}, u32[]{:S(2)}, u32[]{:S(2)}) collective-permute-start(f32[32,3,512]{2,1,0:T(4,128)S(1)} %pad_maximum_fusion), channel_id=1, source_target_pairs={{0,1},{1,2},{2,3},{4,5},{5,6},{6,7},{8,9},{9,10},{10,11},{12,13},{... | collective-permute-start | bytes 589832 | tf_op jit(solution)/shard_map/ppermute | solution.py:14
  104.1 3.9 %copy-start.2 = (f32[32,32,512]{2,1,0:T(8,128)S(1)}, f32[32,32,512]{2,1,0:T(8,128)}, u32[]{:S(2)}) copy-start(f32[32,32,512]{2,1,0:T(8,128)} %param.12) | copy-start | bytes 6291460
  104.1 74.8 %all-to-all-start.1 = ((bf16[32,48,1024]{2,1,0:T(8,128)(2,1)}), bf16[32,48,1024]{2,1,0:T(8,128)(2,1)}, u32[]{:S(2)}, u32[]{:S(2)}) async-start(bf16[32,48,1024]{2,1,0:T(8,128)(2,1)} %bitcast.126), calls=%async_computation.1 | async-start | bytes 6291456 | tf_op jit(solution)/shard_map/all_to_all | solution.py:55
  121.0 2.0 copy-start.6
  183.7 6.0 %copy-start.11 = (f32[31,32,512]{2,1,0:T(8,128)S(1)}, f32[31,32,512]{2,1,0:T(8,128)}, u32[]{:S(2)}) copy-start(f32[31,32,512]{2,1,0:T(8,128)} %slice.176) | copy-start | bytes 6094852
  189.2 2.2 %copy-start.4 = (f32[32,32,512]{2,1,0:T(8,128)S(1)}, f32[32,32,512]{2,1,0:T(8,128)}, u32[]{:S(2)}) copy-start(f32[32,32,512]{2,1,0:T(8,128)} %get-tuple-element.42) | copy-start | bytes 6291460
  189.2 2.8 %copy-start.5 = (f32[32,32,512]{2,1,0:T(8,128)S(1)}, f32[32,32,512]{2,1,0:T(8,128)}, u32[]{:S(2)}) copy-start(f32[32,32,512]{2,1,0:T(8,128)} %get-tuple-element.43) | copy-start | bytes 6291460
  189.2 3.4 %copy-start.7 = (f32[32,32,512]{2,1,0:T(8,128)S(1)}, f32[32,32,512]{2,1,0:T(8,128)}, u32[]{:S(2)}) copy-start(f32[32,32,512]{2,1,0:T(8,128)} %copy-done.6) | copy-start | bytes 6291460
  195.2 5.1 %collective-permute-start.5 = (f32[1,32,512]{2,1,0:T(8,128)S(1)}, f32[1,32,512]{2,1,0:T(8,128)S(1)}, u32[]{:S(2)}, u32[]{:S(2)}) collective-permute-start(f32[1,32,512]{2,1,0:T(8,128)S(1)} %slice.182), channel_id=1, source_target_pairs={{0,4},{4,8},{8,12},{12,16},{16,20},{20,24},{24,28},{1,5},{5,9},{9,... | collective-permute-start | bytes 196616 | tf_op jit(solution)/shard_map/ppermute | solution.py:14
  196.8 5.3 %collective-permute-start.7 = (f32[32,1,512]{2,1,0:T(1,128)S(1)}, f32[32,1,512]{2,1,0:T(1,128)S(1)}, u32[]{:S(2)}, u32[]{:S(2)}) collective-permute-start(f32[32,1,512]{2,1,0:T(1,128)S(1)} %slice.186), channel_id=1, source_target_pairs={{0,1},{1,2},{2,3},{4,5},{5,6},{6,7},{8,9},{9,10},{10,11},{12,13},{... | collective-permute-start | bytes 196616 | tf_op jit(solution)/shard_map/ppermute | solution.py:14
  200.3 4.5 %collective-permute-start.4 = (f32[1,32,512]{2,1,0:T(8,128)S(1)}, f32[1,32,512]{2,1,0:T(8,128)S(1)}, u32[]{:S(2)}, u32[]{:S(2)}) collective-permute-start(f32[1,32,512]{2,1,0:T(8,128)S(1)} %get-tuple-element.48), channel_id=1, source_target_pairs={{4,0},{8,4},{12,8},{16,12},{20,16},{24,20},{28,24},{5,1},{9,5},{13... | collective-permute-start | bytes 196616 | tf_op jit(solution)/shard_map/ppermute | solution.py:14
  202.3 6.5 %collective-permute-start.6 = (f32[32,1,512]{2,1,0:T(1,128)S(1)}, f32[32,1,512]{2,1,0:T(1,128)S(1)}, u32[]{:S(2)}, u32[]{:S(2)}) collective-permute-start(f32[32,1,512]{2,1,0:T(1,128)S(1)} %get-tuple-element.46), channel_id=1, source_target_pairs={{1,0},{2,1},{3,2},{5,4},{6,5},{7,6},{9,8},{10,9},{11,10},{13,12},{... | collective-permute-start | bytes 196616 | tf_op jit(solution)/shard_map/ppermute | solution.py:14
  211.6 4.0 %copy-start.8 = (f32[32,32,512]{2,1,0:T(8,128)}, f32[32,32,512]{2,1,0:T(8,128)S(1)}, u32[]{:S(2)}) copy-start(f32[32,32,512]{2,1,0:T(8,128)S(1)} %get-tuple-element.37) | copy-start | bytes 6291460
  211.6 4.0 %copy-start.9 = (f32[32,32,512]{2,1,0:T(8,128)}, f32[32,32,512]{2,1,0:T(8,128)S(1)}, u32[]{:S(2)}) copy-start(f32[32,32,512]{2,1,0:T(8,128)S(1)} %get-tuple-element.38) | copy-start | bytes 6291460
  211.6 3.9 %copy-start.10 = (f32[32,32,512]{2,1,0:T(8,128)}, f32[32,32,512]{2,1,0:T(8,128)S(1)}, u32[]{:S(2)}) copy-start(f32[32,32,512]{2,1,0:T(8,128)S(1)} %get-tuple-element.39) | copy-start | bytes 6291460
  211.9 3.7 %copy-start.1 = (bf16[16,32,512]{2,1,0:T(8,128)(2,1)S(1)}, bf16[16,32,512]{2,1,0:T(8,128)(2,1)}, u32[]{:S(2)}) copy-start(bf16[16,32,512]{2,1,0:T(8,128)(2,1)} %param.20) | copy-start | bytes 1572868
  (1 other events, 1.6 us)
where the time goes:
time: 217 us; the launch traced here: 216 us
  blocking collectives  67.1 us (31%)
  waiting for transfers between devices  60.3 us (28%)
  starting transfers between devices  28.1 us (13%)
  other arithmetic  24.9 us (11%)
  local copies, waits for them, and re-layouts  24.5 us (11%)
  matrix products  9.48 us (4%)
    all_gather x1, blocking collectives, bubble_source(): lax.all_gather(code, ('gx', 'gy'), axis=0, tiled=True)  67.1 us
    all_to_all x1, waiting for transfers between devices, bubble_source(): lax.all_to_all(outgoing.reshape(devices, capacity, steps * depth), ('gx',...  55.8 us
    ppermute x8, starting transfers between devices, from_behind(): return lax.ppermute(block, axis, route)  17.9 us
    sub x2, other arithmetic, body(): vel_z = vel_z - step_ratio * buoyancy * (next_z - pressure)  10.5 us
    all_to_all x1, starting transfers between devices, incident_plane(): rows = lax.all_to_all(chosen, 'gx', split_axis=0, concat_axis=0, tiled=True)  6.32 us
    add x2, other arithmetic, body(): pressure + step_ratio * stiffness * (source[:, :, step, :] + forcing - di...  6.18 us
    dot_general x1, matrix products, bubble_source(): jnp.dot(hits, incoming.reshape(slots, steps * depth), preferred_element_t...  5.48 us
    reshape x1, local copies, waits for them, and re-layouts, bubble_source(): incoming.reshape(slots, steps * depth)  4.69 us
  transfers between devices with their start and end apart: 10, of which 3 were waited for; matrix products, arithmetic and copies ran while one was open for 16% of the time, Pallas kernels for 0%

commit v1 on v0

--- a/solution.py
+++ b/solution.py
@@ -6,6 +6,20 @@
 step_ratio = 0.4
 gas_density = 0.001
 gas_stiffness = 5.29e-05
+
+
+def place_gates(on_dim, my_data):
+    x_next, x_new = (jax.lax.axis_size(("gx", "gy")), jax.lax.axis_index(("gx", "gy")))
+    y2, high = (my_data, 1)
+    while high < x_next:
+        mat_out = jax.lax.ppermute(
+            y2, ("gx", "gy"), [(to_i, to_i ^ high) for to_i in range(x_next)]
+        )
+        taken_in = jnp.concatenate([y2, mat_out], on_dim)
+        then = jnp.concatenate([mat_out, y2], on_dim)
+        y2 = jnp.where(x_new & high == 0, taken_in, then)
+        high = 2 * high
+    return y2
 
 
 def from_behind(block, axis, distance):
@@ -42,7 +56,7 @@
         preferred_element_type=jnp.float32,
     ).astype(jnp.bfloat16)
     code = dest * cells + bubble_column
-    all_code = lax.all_gather(code, ("gx", "gy"), axis=0, tiled=True).reshape(devices, bubbles)
+    all_code = place_gates(0, code).reshape(devices, bubbles)
     all_dest = all_code // cells
     all_col = all_code % cells
     mine = (all_dest == me).astype(jnp.int32)

time: 217 us -> 168 us (0.77)
  blocking collectives: 67.1 us -> 0 us
  starting transfers between devices: 28.1 us -> 38.2 us
  waiting for transfers between devices: 60.3 us -> 67.3 us
    all_gather x1 -> x0, blocking collectives: 67.1 us -> none  [bubble_source(): lax.all_gather(code, ('gx', 'gy'), axis=0, tiled=True)]
    ppermute x0 -> x5, starting transfers between devices: none -> 9.66 us  [place_gates(): jax.lax.ppermute(y2, ('gx', 'gy'), [(to_i, to_i ^ high) for to_i in range...]
    ppermute x0 -> x5, waiting for transfers between devices: none -> 7 us  [place_gates(): jax.lax.ppermute(y2, ('gx', 'gy'), [(to_i, to_i ^ high) for to_i in range...]
  transfers between devices with their start and end apart: 10 -> 15, of which waited for: 3 -> 7; matrix products, arithmetic and copies ran while one was open for 16% -> 20% of each run, Pallas kernels for 0% -> 0%
where the time goes in v1:
time: 168 us; the launch traced here: 167 us
  waiting for transfers between devices  67.3 us (40%)
  starting transfers between devices  38.2 us (23%)
  other arithmetic  26.3 us (16%)
  local copies, waits for them, and re-layouts  24.5 us (15%)
  matrix products  9.47 us (6%)
    all_to_all x1, waiting for transfers between devices, bubble_source(): lax.all_to_all(outgoing.reshape(devices, capacity, steps * depth), ('gx',...  55.8 us
    ppermute x8, starting transfers between devices, from_behind(): return lax.ppermute(block, axis, route)  17.7 us
    sub x2, other arithmetic, body(): vel_z = vel_z - step_ratio * buoyancy * (next_z - pressure)  10.5 us
    ppermute x5, starting transfers between devices, place_gates(): jax.lax.ppermute(y2, ('gx', 'gy'), [(to_i, to_i ^ high) for to_i in range...  9.66 us
    ppermute x5, waiting for transfers between devices, place_gates(): jax.lax.ppermute(y2, ('gx', 'gy'), [(to_i, to_i ^ high) for to_i in range...  7 us
    add x2, other arithmetic, body(): pressure + step_ratio * stiffness * (source[:, :, step, :] + forcing - di...  6.18 us
    all_to_all x1, starting transfers between devices, bubble_source(): lax.all_to_all(outgoing.reshape(devices, capacity, steps * depth), ('gx',...  5.93 us
    dot_general x1, matrix products, bubble_source(): jnp.dot(hits, incoming.reshape(slots, steps * depth), preferred_element_t...  5.48 us
  transfers between devices with their start and end apart: 15, of which 7 were waited for; matrix products, arithmetic and copies ran while one was open for 20% of the time, Pallas kernels for 0%

profile of v1, /device:TPU:0, one launch (start us, length us, event | category | flops | bytes accessed | tf_op | source)
XLA Modules:
  0.0 167.2 jit_solution(10494521352324703895)
XLA Ops:
  1.5 1.7 %reduce-window.16 = s32[32,6,128]{2,0,1:T(8,128)S(1)} reduce-window(s32[32,6,128]{2,0,1:T(8,128)S(1)} %fusion.34, s32[]{:T(128)} %constant.126.clone.1), window={size=1x1x128 pad=0_0x0_0x127_0}, to_apply=%region_3.4 | reduce-window | flops 3121152 | bytes 196612 | tf_op jit(solution)/shard_map/reduce-window.2
  4.4 2.9 %collective-permute-start = (s32[768]{0:T(1024)S(1)}, s32[768]{0:T(1024)S(1)}, u32[]{:S(2)}, u32[]{:S(2)}) collective-permute-start(s32[768]{0:T(1024)S(1)} %get-tuple-element.56), channel_id=1, source_target_pairs={{0,1},{1,0},{2,3},{3,2},{4,5},{5,4},{6,7},{7,6},{8,9},{9,8},{10,11... | collective-permute-start | bytes 9224 | tf_op jit(solution)/shard_map/ppermute | solution.py:15
  13.8 3.0 %collective-permute-start.7 = (f32[3,32,512]{2,1,0:T(8,128)S(1)}, f32[3,32,512]{2,1,0:T(8,128)S(1)}, u32[]{:S(2)}, u32[]{:S(2)}) collective-permute-start(f32[3,32,512]{2,1,0:T(8,128)S(1)} %pad_maximum_fusion.1), channel_id=1, source_target_pairs={{0,4},{4,8},{8,12},{12,16},{16,20},{20,24},{24,28},{1,5},{5,9},{9,... | collective-permute-start | bytes 589832 | tf_op jit(solution)/shard_map/ppermute | solution.py:28
  20.0 4.9 %all-to-all-start = ((bf16[8,32,512]{2,1,0:T(8,128)(2,1)}), bf16[8,32,512]{2,1,0:T(8,128)(2,1)S(1)}, u32[]{:S(2)}, u32[]{:S(2)}) async-start(bf16[8,32,512]{2,1,0:T(8,128)(2,1)} %broadcast_select_fusion), calls=%async_computation | async-start | bytes 524288 | tf_op jit(solution)/shard_map/all_to_all | solution.py:94
  27.3 4.6 %collective-permute-start.8 = (f32[32,3,512]{2,1,0:T(4,128)S(1)}, f32[32,3,512]{2,1,0:T(4,128)S(1)}, u32[]{:S(2)}, u32[]{:S(2)}) collective-permute-start(f32[32,3,512]{2,1,0:T(4,128)S(1)} %pad_maximum_fusion), channel_id=1, source_target_pairs={{0,1},{1,2},{2,3},{4,5},{5,6},{6,7},{8,9},{9,10},{10,11},{12,13},{... | collective-permute-start | bytes 589832 | tf_op jit(solution)/shard_map/ppermute | solution.py:28
  32.3 4.0 %fusion.4 = bf16[1536,1024]{1,0:T(8,128)(2,1)} fusion(bf16[768,1024]{1,0:T(8,128)(2,1)S(1)} %bitcast.80, s32[768]{0:T(1024)S(1)} %get-tuple-element.55), kind=kOutput, calls=%fused_computation.8 | convolution fusion | flops 2418671616 | bytes 4721664 | tf_op jit(solution)/shard_map/dot_general | solution.py:53
  37.9 2.1 %collective-permute-done.1 = s32[1536]{0:T(1024)S(1)} collective-permute-done((s32[1536]{0:T(1024)S(1)}, s32[1536]{0:T(1024)S(1)}, u32[]{:S(2)}, u32[]{:S(2)}) %collective-permute-start.1) | collective-permute-done | bytes 6176 | tf_op jit(solution)/shard_map/ppermute | solution.py:15
  41.3 2.1 %collective-permute-start.3 = (s32[6144]{0:T(1024)S(1)}, s32[6144]{0:T(1024)S(1)}, u32[]{:S(2)}, u32[]{:S(2)}) collective-permute-start(s32[6144]{0:T(1024)S(1)} %add_select_fusion.9), channel_id=1, source_target_pairs={{0,8},{1,9},{2,10},{3,11},{4,12},{5,13},{6,14},{7,15},{8,0},{9,1},... | collective-permute-start | bytes 73736 | tf_op jit(solution)/shard_map/ppermute | solution.py:15
  43.4 1.8 %collective-permute-done.3 = s32[6144]{0:T(1024)S(1)} collective-permute-done((s32[6144]{0:T(1024)S(1)}, s32[6144]{0:T(1024)S(1)}, u32[]{:S(2)}, u32[]{:S(2)}) %collective-permute-start.3) | collective-permute-done | bytes 24608 | tf_op jit(solution)/shard_map/ppermute | solution.py:15
  45.2 3.0 %collective-permute-start.4 = (s32[12288]{0:T(1024)S(1)}, s32[12288]{0:T(1024)S(1)}, u32[]{:S(2)}, u32[]{:S(2)}) collective-permute-start(s32[12288]{0:T(1024)S(1)} %add_select_fusion.6), channel_id=1, source_target_pairs={{0,16},{1,17},{2,18},{3,19},{4,20},{5,21},{6,22},{7,23},{8,24},{9,... | collective-permute-start | bytes 147464 | tf_op jit(solution)/shard_map/ppermute | solution.py:15
  48.2 2.1 %collective-permute-done.4 = s32[12288]{0:T(1024)S(1)} collective-permute-done((s32[12288]{0:T(1024)S(1)}, s32[12288]{0:T(1024)S(1)}, u32[]{:S(2)}, u32[]{:S(2)}) %collective-permute-start.4) | collective-permute-done | bytes 49184 | tf_op jit(solution)/shard_map/ppermute | solution.py:15
  50.4 1.7 %reduce-window.14 = s32[32,6,128]{2,0,1:T(8,128)S(1)} reduce-window(s32[32,6,128]{2,0,1:T(8,128)S(1)} %fusion.35, s32[]{:T(128)} %constant.126.clone.1), window={size=1x1x128 pad=0_0x0_0x127_0}, to_apply=%region_0.1 | reduce-window | flops 3121152 | bytes 196612 | tf_op jit(solution)/shard_map/reduce-window
  53.6 5.9 %all-to-all-start.1 = ((bf16[32,48,1024]{2,1,0:T(8,128)(2,1)}), bf16[32,48,1024]{2,1,0:T(8,128)(2,1)}, u32[]{:S(2)}, u32[]{:S(2)}) async-start(bf16[32,48,1024]{2,1,0:T(8,128)(2,1)} %bitcast.77), calls=%async_computation.1 | async-start | bytes 6291456 | tf_op jit(solution)/shard_map/all_to_all | solution.py:69
  61.1 1.7 %slice.153 = f32[32,31,512]{2,1,0:T(8,128)} slice(f32[32,32,512]{2,1,0:T(8,128)S(1)} %copy-done.2), slice={[0:32], [1:32], [0:512]} | slice | bytes 4063232 | tf_op jit(solution)/shard_map/slice | solution.py:127
  62.8 1.9 %slice.158 = f32[32,32,511]{2,1,0:T(8,128)} slice(f32[32,32,512]{2,1,0:T(8,128)S(1)} %copy-done.2), slice={[0:32], [0:32], [1:512]} | slice | bytes 4186112 | tf_op jit(solution)/shard_map/slice | solution.py:128
  64.8 7.7 %multiply_subtract_fusion.1 = (f32[32,32,512]{2,1,0:T(8,128)}, f32[32,32,512]{2,1,0:T(8,128)}, f32[32,32,512]{2,1,0:T(8,128)S(1)}) fusion(f32[32,32,512]{2,1,0:T(8,128)} %param.15, f32[32,32,512]{2,1,0:T(8,128)S(1)} %copy-done.2, f32[32,32,511]{2,1,0:T(8,128)} %slice.158, f32[32,32,512]{2,1,0:T(8,128)} %param.16, f32[32,32,512]{2,1,0:T(8,128)} %param.14, ...), kind=kLoop, calls=%fused_computation.41 | loop fusion | flops 8388608 | bytes 23064576 | tf_op jit(solution)/shard_map/sub | solution.py:131
  74.7 55.8 %all-to-all-done.1 = bf16[32,48,1024]{2,1,0:T(8,128)(2,1)} async-done(((bf16[32,48,1024]{2,1,0:T(8,128)(2,1)}), bf16[32,48,1024]{2,1,0:T(8,128)(2,1)}, u32[]{:S(2)}, u32[]{:S(2)}) %all-to-all-start.1) | async-done | bytes 3145760 | tf_op jit(solution)/shard_map/all_to_all | solution.py:69
  130.5 4.6 %copy.42 = bf16[1536,1024]{0,1:T(8,128)(2,1)} copy(bf16[1536,1024]{1,0:T(8,128)(2,1)} %bitcast.4) | data formatting | bytes 6291456 | tf_op jit(solution)/shard_map/reshape | solution.py:80
  135.1 5.5 %fusion = f32[32,32,2,512]{3,1,2,0:T(8,128)S(1)} fusion(bf16[2,512,1536,1]{2,1,0,3:T(8,128)(2,1)} %bitcast.78, s32[1536]{0:T(1024)S(1)} %eq.133, s32[32,32]{1,0:T(8,128)S(1)} %multiply_add_fusion), kind=kOutput, calls=%fused_computation.1 | convolution fusion | flops 3222798336 | bytes 7350272 | tf_op jit(solution)/shard_map/dot_general | solution.py:79
  144.1 2.5 %fusion.14 = f32[32,32,512]{2,1,0:T(8,128)S(1)} fusion(f32[32,32,512]{2,1,0:T(8,128)S(1)} %copy-done.2, f32[32,32,512]{2,1,0:T(8,128)S(1)} %get-tuple-element.36, f32[32,32,512]{2,1,0:T(8,128)S(1)} %copy-done.7, f32[31,32,512]{2,1,0:T(8,128)S(1)} %copy-done.11, f32[1,32,512]{2,1,0:T(8,128)S(1)} %get-tuple-element.33, f32[32,32,512]{2,1,0:T(8,128)S(1)} %copy-done.5, ...), kind=kLoop, calls=%fused_computation.22 | loop fusion | flops 7864320 | bytes 20967424 | tf_op jit(solution)/shard_map/add | solution.py:140
  148.3 3.4 %collective-permute-start.12 = (f32[32,1,512]{2,1,0:T(1,128)S(1)}, f32[32,1,512]{2,1,0:T(1,128)S(1)}, u32[]{:S(2)}, u32[]{:S(2)}) collective-permute-start(f32[32,1,512]{2,1,0:T(1,128)S(1)} %slice.186), channel_id=1, source_target_pairs={{0,1},{1,2},{2,3},{4,5},{5,6},{6,7},{8,9},{9,10},{10,11},{12,13},{... | collective-permute-start | bytes 196616 | tf_op jit(solution)/shard_map/ppermute | solution.py:28
  156.3 4.0 %collective-permute-done.11 = f32[32,1,512]{2,1,0:T(1,128)S(1)} collective-permute-done((f32[32,1,512]{2,1,0:T(1,128)S(1)}, f32[32,1,512]{2,1,0:T(1,128)S(1)}, u32[]{:S(2)}, u32[]{:S(2)}) %collective-permute-start.11) | collective-permute-done | bytes 65568 | tf_op jit(solution)/shard_map/ppermute | solution.py:28
  160.3 2.8 %multiply_subtract_fusion = (f32[32,32,512]{2,1,0:T(8,128)S(1)}, f32[32,32,512]{2,1,0:T(8,128)S(1)}, f32[32,32,512]{2,1,0:T(8,128)S(1)}) fusion(f32[32,32,512]{2,1,0:T(8,128)S(1)} %copy-done.4, f32[32,32,512]{2,1,0:T(8,128)S(1)} %fusion.14, f32[32,32,511]{2,1,0:T(8,128)S(1)} %slice.188, f32[32,32,512]{2,1,0:T(8,128)S(1)} %copy-done.3, ...), kind=kLoop, calls=%fused_computation.40 | loop fusion | flops 8388608 | bytes 23064576 | tf_op jit(solution)/shard_map/sub | solution.py:131
  163.4 3.6 %fusion.23 = f32[32,32,512]{2,1,0:T(8,128)} fusion(f32[32,32,512]{2,1,0:T(8,128)S(1)} %fusion.14, f32[32,32,512]{2,1,0:T(8,128)S(1)} %get-tuple-element.35, f32[32,32,512]{2,1,0:T(8,128)S(1)} %get-tuple-element.39, f32[31,32,512]{2,1,0:T(8,128)S(1)} %slice.183, f32[1,32,512]{2,1,0:T(8,128)S(1)} %get-tuple-element.47, ...), kind=kLoop, calls=%fused_computation.35 | loop fusion | flops 7864320 | bytes 20967424 | tf_op jit(solution)/shard_map/add | solution.py:140
  (112 shorter events, 32.4 us)
Async XLA Ops:
  0.6 18.0 %copy-start = (bf16[16,32,512]{2,1,0:T(8,128)(2,1)S(1)}, bf16[16,32,512]{2,1,0:T(8,128)(2,1)}, u32[]{:S(2)}) copy-start(bf16[16,32,512]{2,1,0:T(8,128)(2,1)} %param.20) | copy-start | bytes 1572868
  0.6 31.2 %copy-start.12 = (bf16[768,2,512]{2,1,0:T(2,128)(2,1)S(1)}, bf16[768,2,512]{2,1,0:T(2,128)(2,1)}, u32[]{:S(2)}) copy-start(bf16[768,2,512]{2,1,0:T(2,128)(2,1)} %param.17) | copy-start | bytes 4718596
  4.4 31.9 %collective-permute-start = (s32[768]{0:T(1024)S(1)}, s32[768]{0:T(1024)S(1)}, u32[]{:S(2)}, u32[]{:S(2)}) collective-permute-start(s32[768]{0:T(1024)S(1)} %get-tuple-element.56), channel_id=1, source_target_pairs={{0,1},{1,0},{2,3},{3,2},{4,5},{5,4},{6,7},{7,6},{8,9},{9,8},{10,11... | collective-permute-start | bytes 9224 | tf_op jit(solution)/shard_map/ppermute | solution.py:15
  8.6 44.9 %collective-permute-start.6 = (f32[32,1,512]{2,1,0:T(1,128)S(1)}, f32[32,1,512]{2,1,0:T(1,128)S(1)}, u32[]{:S(2)}, u32[]{:S(2)}) collective-permute-start(f32[32,1,512]{2,1,0:T(1,128)S(1)} %get-tuple-element.50), channel_id=1, source_target_pairs={{1,0},{2,1},{3,2},{5,4},{6,5},{7,6},{9,8},{10,9},{11,10},{13,12},{... | collective-permute-start | bytes 196616 | tf_op jit(solution)/shard_map/ppermute | solution.py:28
  10.8 42.7 %collective-permute-start.5 = (f32[1,32,512]{2,1,0:T(8,128)S(1)}, f32[1,32,512]{2,1,0:T(8,128)S(1)}, u32[]{:S(2)}, u32[]{:S(2)}) collective-permute-start(f32[1,32,512]{2,1,0:T(8,128)S(1)} %get-tuple-element.52), channel_id=1, source_target_pairs={{4,0},{8,4},{12,8},{16,12},{20,16},{24,20},{28,24},{5,1},{9,5},{13... | collective-permute-start | bytes 196616 | tf_op jit(solution)/shard_map/ppermute | solution.py:28
  13.8 39.7 %collective-permute-start.7 = (f32[3,32,512]{2,1,0:T(8,128)S(1)}, f32[3,32,512]{2,1,0:T(8,128)S(1)}, u32[]{:S(2)}, u32[]{:S(2)}) collective-permute-start(f32[3,32,512]{2,1,0:T(8,128)S(1)} %pad_maximum_fusion.1), channel_id=1, source_target_pairs={{0,4},{4,8},{8,12},{12,16},{16,20},{20,24},{24,28},{1,5},{5,9},{9,... | collective-permute-start | bytes 589832 | tf_op jit(solution)/shard_map/ppermute | solution.py:28
  20.0 33.4 %all-to-all-start = ((bf16[8,32,512]{2,1,0:T(8,128)(2,1)}), bf16[8,32,512]{2,1,0:T(8,128)(2,1)S(1)}, u32[]{:S(2)}, u32[]{:S(2)}) async-start(bf16[8,32,512]{2,1,0:T(8,128)(2,1)} %broadcast_select_fusion), calls=%async_computation | async-start | bytes 524288 | tf_op jit(solution)/shard_map/all_to_all | solution.py:94
  27.3 26.3 %collective-permute-start.8 = (f32[32,3,512]{2,1,0:T(4,128)S(1)}, f32[32,3,512]{2,1,0:T(4,128)S(1)}, u32[]{:S(2)}, u32[]{:S(2)}) collective-permute-start(f32[32,3,512]{2,1,0:T(4,128)S(1)} %pad_maximum_fusion), channel_id=1, source_target_pairs={{0,1},{1,2},{2,3},{4,5},{5,6},{6,7},{8,9},{9,10},{10,11},{12,13},{... | collective-permute-start | bytes 589832 | tf_op jit(solution)/shard_map/ppermute | solution.py:28
  36.3 3.7 %collective-permute-start.1 = (s32[1536]{0:T(1024)S(1)}, s32[1536]{0:T(1024)S(1)}, u32[]{:S(2)}, u32[]{:S(2)}) collective-permute-start(s32[1536]{0:T(1024)S(1)} %add_select_fusion.14), channel_id=1, source_target_pairs={{0,2},{1,3},{2,0},{3,1},{4,6},{5,7},{6,4},{7,5},{8,10},{9,11},{10,... | collective-permute-start | bytes 18440 | tf_op jit(solution)/shard_map/ppermute | solution.py:15
  40.0 1.2 collective-permute-start.2
  41.3 3.9 %collective-permute-start.3 = (s32[6144]{0:T(1024)S(1)}, s32[6144]{0:T(1024)S(1)}, u32[]{:S(2)}, u32[]{:S(2)}) collective-permute-start(s32[6144]{0:T(1024)S(1)} %add_select_fusion.9), channel_id=1, source_target_pairs={{0,8},{1,9},{2,10},{3,11},{4,12},{5,13},{6,14},{7,15},{8,0},{9,1},... | collective-permute-start | bytes 73736 | tf_op jit(solution)/shard_map/ppermute | solution.py:15
  45.2 5.1 %collective-permute-start.4 = (s32[12288]{0:T(1024)S(1)}, s32[12288]{0:T(1024)S(1)}, u32[]{:S(2)}, u32[]{:S(2)}) collective-permute-start(s32[12288]{0:T(1024)S(1)} %add_select_fusion.6), channel_id=1, source_target_pairs={{0,16},{1,17},{2,18},{3,19},{4,20},{5,21},{6,22},{7,23},{8,24},{9,... | collective-permute-start | bytes 147464 | tf_op jit(solution)/shard_map/ppermute | solution.py:15
  53.6 6.0 %copy-start.2 = (f32[32,32,512]{2,1,0:T(8,128)S(1)}, f32[32,32,512]{2,1,0:T(8,128)}, u32[]{:S(2)}) copy-start(f32[32,32,512]{2,1,0:T(8,128)} %param.12) | copy-start | bytes 6291460
  53.6 76.9 %all-to-all-start.1 = ((bf16[32,48,1024]{2,1,0:T(8,128)(2,1)}), bf16[32,48,1024]{2,1,0:T(8,128)(2,1)}, u32[]{:S(2)}, u32[]{:S(2)}) async-start(bf16[32,48,1024]{2,1,0:T(8,128)(2,1)} %bitcast.77), calls=%async_computation.1 | async-start | bytes 6291456 | tf_op jit(solution)/shard_map/all_to_all | solution.py:69
  135.1 6.0 %copy-start.11 = (f32[31,32,512]{2,1,0:T(8,128)S(1)}, f32[31,32,512]{2,1,0:T(8,128)}, u32[]{:S(2)}) copy-start(f32[31,32,512]{2,1,0:T(8,128)} %slice.176) | copy-start | bytes 6094852
  140.7 3.4 %copy-start.7 = (f32[32,32,512]{2,1,0:T(8,128)S(1)}, f32[32,32,512]{2,1,0:T(8,128)}, u32[]{:S(2)}) copy-start(f32[32,32,512]{2,1,0:T(8,128)} %copy-done.6) | copy-start | bytes 6291460
  146.7 5.0 %collective-permute-start.10 = (f32[1,32,512]{2,1,0:T(8,128)S(1)}, f32[1,32,512]{2,1,0:T(8,128)S(1)}, u32[]{:S(2)}, u32[]{:S(2)}) collective-permute-start(f32[1,32,512]{2,1,0:T(8,128)S(1)} %slice.182), channel_id=1, source_target_pairs={{0,4},{4,8},{8,12},{12,16},{16,20},{20,24},{24,28},{1,5},{5,9},{9,... | collective-permute-start | bytes 196616 | tf_op jit(solution)/shard_map/ppermute | solution.py:28
  148.3 5.3 %collective-permute-start.12 = (f32[32,1,512]{2,1,0:T(1,128)S(1)}, f32[32,1,512]{2,1,0:T(1,128)S(1)}, u32[]{:S(2)}, u32[]{:S(2)}) collective-permute-start(f32[32,1,512]{2,1,0:T(1,128)S(1)} %slice.186), channel_id=1, source_target_pairs={{0,1},{1,2},{2,3},{4,5},{5,6},{6,7},{8,9},{9,10},{10,11},{12,13},{... | collective-permute-start | bytes 196616 | tf_op jit(solution)/shard_map/ppermute | solution.py:28
  151.8 4.5 %collective-permute-start.9 = (f32[1,32,512]{2,1,0:T(8,128)S(1)}, f32[1,32,512]{2,1,0:T(8,128)S(1)}, u32[]{:S(2)}, u32[]{:S(2)}) collective-permute-start(f32[1,32,512]{2,1,0:T(8,128)S(1)} %get-tuple-element.48), channel_id=1, source_target_pairs={{4,0},{8,4},{12,8},{16,12},{20,16},{24,20},{28,24},{5,1},{9,5},{13... | collective-permute-start | bytes 196616 | tf_op jit(solution)/shard_map/ppermute | solution.py:28
  153.7 6.5 %collective-permute-start.11 = (f32[32,1,512]{2,1,0:T(1,128)S(1)}, f32[32,1,512]{2,1,0:T(1,128)S(1)}, u32[]{:S(2)}, u32[]{:S(2)}) collective-permute-start(f32[32,1,512]{2,1,0:T(1,128)S(1)} %get-tuple-element.46), channel_id=1, source_target_pairs={{1,0},{2,1},{3,2},{5,4},{6,5},{7,6},{9,8},{10,9},{11,10},{13,12},{... | collective-permute-start | bytes 196616 | tf_op jit(solution)/shard_map/ppermute | solution.py:28
  163.1 4.0 %copy-start.8 = (f32[32,32,512]{2,1,0:T(8,128)}, f32[32,32,512]{2,1,0:T(8,128)S(1)}, u32[]{:S(2)}) copy-start(f32[32,32,512]{2,1,0:T(8,128)S(1)} %get-tuple-element.37) | copy-start | bytes 6291460
  163.1 4.0 %copy-start.9 = (f32[32,32,512]{2,1,0:T(8,128)}, f32[32,32,512]{2,1,0:T(8,128)S(1)}, u32[]{:S(2)}) copy-start(f32[32,32,512]{2,1,0:T(8,128)S(1)} %get-tuple-element.38) | copy-start | bytes 6291460
  163.1 3.9 %copy-start.10 = (f32[32,32,512]{2,1,0:T(8,128)}, f32[32,32,512]{2,1,0:T(8,128)S(1)}, u32[]{:S(2)}) copy-start(f32[32,32,512]{2,1,0:T(8,128)S(1)} %get-tuple-element.39) | copy-start | bytes 6291460
  163.4 3.7 %copy-start.1 = (bf16[16,32,512]{2,1,0:T(8,128)(2,1)S(1)}, bf16[16,32,512]{2,1,0:T(8,128)(2,1)}, u32[]{:S(2)}) copy-start(bf16[16,32,512]{2,1,0:T(8,128)(2,1)} %param.20) | copy-start | bytes 1572868
  (4 other events, 8.6 us)
